TPU v7x, 512 devices: a whole 4x8x8 slice. The times are simulated.
512 devices in a mesh: island: 64 (over z, x, y_hi), fsdp: 8 (over y_lo, core).
Axes of the slice: x: 4, y: 8 (y_hi: 2, y_lo: 4; y = y_hi * 4 + y_lo), z: 8, core: 2. Of those that a mesh axis runs over, the one named last changes fastest.
Arguments:
- hidden: bfloat16 [64, 1024, 8192], P('island', 'fsdp'), may hold values from -6 to 6
- gain: bfloat16 [8192], P('fsdp'), may hold values from 0.5 to 1.5
- doc_ids: int32 [64, 1024], P('island', 'fsdp'), may hold values from 0 to 7, never falling along the last dimension, each value on 1 to 256 neighbouring positions
- cotangent: bfloat16 [64, 1024, 512], P('island', 'fsdp'), may hold values from -0.1796875 to 0.1796875
- pseudo_grad: bfloat16 [64, 8192, 512], P('island', 'fsdp'), may hold values from -0.75 to 0.75
- outer_weight: float32 [8192, 512], P(('fsdp', 'island')), may hold values from -0.0625 to 0.0625
- momentum: float32 [8192, 512], P(('fsdp', 'island')), may hold values from -0.0625 to 0.0625
Outputs:
- keys: bfloat16 [64, 1024, 512], P('island', 'fsdp')
- grad_weight: bfloat16 [64, 8192, 512], P('island', 'fsdp')
- grad_gain: float32 [64, 8192], P('island', 'fsdp')
- new_outer: float32 [8192, 512], P(('fsdp', 'island'))
- new_momentum: float32 [8192, 512], P(('fsdp', 'island'))
Inputs may be any that keep to these rules, and one draw needn't show every extreme that they name: `doc_ids`: document numbers never fall along a replica's sequence; every document holds 1 to 256 tokens, and one holds exactly 256.
All inputs are finite; a program needn't handle non-finite values.
Results may differ from a plain program's by a relative error of at most 0.014.
Values may be sent and summed in bfloat16 or wider, within the bound.
No kernel may reach another device: no remote copies, remote signals or barrier semaphores. Data moves between devices by JAX's collectives and lax.ppermute only.
A program may use at most 128 MiB of HBM per device.

v0:
```python
import math
import jax
import jax.numpy as jnp
import numpy as np
from jax import lax
from jax.sharding import Mesh
from jax.sharding import PartitionSpec as P

HEAD = 128
DOCS = 8
learn_rate = 0.7
momentum_rate = 0.9
norm_eps = 1e-05
rope_base = 500000.0
far_index = 1 << 30
ISLAND_FACTORS = None


def angles_for(positions, head_width):
    half_width = head_width // 2
    frequency = jnp.exp(
        jnp.arange(half_width, dtype=jnp.float32) * (-2.0 * math.log(rope_base) / head_width)
    )
    phases = positions[:, None] * frequency[None, :]
    return (jnp.cos(phases), jnp.sin(phases))


def rotate(values, cosine, sine_part, sign):
    rows = values.shape[0]
    half_width = cosine.shape[1]
    shaped = values.reshape(rows, -1, 2 * half_width)
    leading = shaped[:, :, :half_width]
    second = shaped[:, :, half_width:]
    cos_b = cosine[:, None, :]
    sin_b = sine_part[:, None, :] * sign
    joined = jnp.concatenate(
        [leading * cos_b - second * sin_b, second * cos_b + leading * sin_b], axis=2
    )
    return joined.reshape(rows, -1)


def body(island_axes, hidden, gain, doc_ids, cotangent, pseudo_grad, outer_weight, momentum):
    islands = 1
    for ax in island_axes:
        islands *= lax.axis_size(ax)
    fsdp_ways = lax.axis_size("fsdp")
    stages = (island_axes[:1], island_axes[1:]) if len(island_axes) > 1 else (island_axes,)
    summed = pseudo_grad[0].astype(jnp.float32)
    for axes in stages:
        summed = lax.psum_scatter(summed, axes, scatter_dimension=0, tiled=True)
    mean_delta = summed / islands
    new_momentum = momentum_rate * momentum + mean_delta
    new_outer = outer_weight - learn_rate * (mean_delta + momentum_rate * new_momentum)
    weight_shard = new_outer.astype(jnp.bfloat16)
    for axes in reversed(stages):
        weight_shard = lax.all_gather(weight_shard, axes, axis=0, tiled=True)
    tok_rows = hidden.shape[1]
    seq = tok_rows * fsdp_ways
    me = lax.axis_index("fsdp")
    all_docs = lax.all_gather(doc_ids[0], "fsdp", axis=0, tiled=True)
    indices = jnp.arange(seq, dtype=jnp.int32)
    documents = jnp.arange(DOCS, dtype=jnp.int32)
    in_document = all_docs[:, None] == documents[None, :]
    starts = jnp.min(jnp.where(in_document, indices[:, None], far_index), axis=0)
    doc_start = jnp.sum(jnp.where(in_document, starts[None, :], 0), axis=1)
    positions = (indices - doc_start).astype(jnp.float32)
    cosine, sine_part = angles_for(positions, HEAD)
    width = hidden.shape[2] // fsdp_ways
    cols_out = cotangent.shape[2]
    outgoing = jnp.concatenate(
        [
            hidden[0].reshape(tok_rows, fsdp_ways, width).transpose(1, 0, 2),
            jnp.broadcast_to(cotangent[0][None], (fsdp_ways, tok_rows, cols_out)),
        ],
        axis=2,
    )
    incoming = lax.all_to_all(outgoing, "fsdp", split_axis=0, concat_axis=0, tiled=True)
    columns = incoming[:, :, :width].reshape(seq, width)
    all_cot = incoming[:, :, width:].reshape(seq, cols_out)
    all_back = rotate(all_cot.astype(jnp.float32), cosine, sine_part, -1.0).astype(jnp.bfloat16)
    hidden_f = hidden[0].astype(jnp.float32)
    row_scale = lax.rsqrt(jnp.mean(hidden_f * hidden_f, axis=1, keepdims=True) + norm_eps)
    all_scales = lax.all_gather(row_scale, "fsdp", axis=0, tiled=True)
    normed_cols = columns.astype(jnp.float32) * all_scales
    act_cols = (normed_cols * gain.astype(jnp.float32)[None, :]).astype(jnp.bfloat16)
    grad_weight = jnp.zeros((act_cols.shape[1], all_back.shape[1]), jnp.float32)
    for block in range(fsdp_ways):
        act_block = act_cols[block * tok_rows : (block + 1) * tok_rows]
        back_block = all_back[block * tok_rows : (block + 1) * tok_rows]
        part = lax.dot_general(
            act_block, back_block, (((0,), (0,)), ((), ())), preferred_element_type=jnp.float32
        )
        grad_weight = grad_weight + part.astype(jnp.bfloat16).astype(jnp.float32)
    hidden_grad = lax.dot_general(
        all_back, weight_shard, (((1,), (1,)), ((), ())), preferred_element_type=jnp.float32
    )
    grad_gain = jnp.sum(hidden_grad * normed_cols, axis=0)
    partial_keys = jnp.dot(act_cols, weight_shard, preferred_element_type=jnp.float32)
    projected = lax.psum_scatter(partial_keys, "fsdp", scatter_dimension=0, tiled=True)
    my_cos = lax.dynamic_slice_in_dim(cosine, me * tok_rows, tok_rows, axis=0)
    my_sin = lax.dynamic_slice_in_dim(sine_part, me * tok_rows, tok_rows, axis=0)
    rotated = rotate(projected, my_cos, my_sin, 1.0).astype(jnp.bfloat16)
    return (
        rotated[None],
        grad_weight.astype(jnp.bfloat16)[None],
        grad_gain[None],
        new_outer,
        new_momentum,
    )


def _island_factors(n):
    if ISLAND_FACTORS is not None:
        return tuple(ISLAND_FACTORS)
    if n == 64:
        return (8, 4, 2)
    return (n,)


def solution(mesh):
    factors = _island_factors(mesh.shape["island"])
    island_axes = tuple((f"island{k}" for k in range(len(factors))))
    devices = np.asarray(mesh.devices).reshape(factors + (mesh.shape["fsdp"],))
    fine = Mesh(devices, island_axes + ("fsdp",))
    isl = island_axes
    placed = (
        P(isl, "fsdp", None),
        P("fsdp"),
        P(isl, "fsdp"),
        P(isl, "fsdp", None),
        P(isl, "fsdp", None),
        P(("fsdp",) + isl, None),
        P(("fsdp",) + isl, None),
    )
    return jax.shard_map(
        lambda *a: body(island_axes, *a),
        mesh=fine,
        in_specs=placed,
        out_specs=(
            P(isl, "fsdp", None),
            P(isl, "fsdp", None),
            P(isl, "fsdp"),
            P(("fsdp",) + isl, None),
            P(("fsdp",) + isl, None),
        ),
        check_vma=False,
    )
```

profile of v0, /device:TPU:6, one launch (start us, length us, event | category | flops | bytes accessed | tf_op | source)
XLA Modules:
  0.0 294.2 jit_solution(8046850983464915095)
XLA Ops:
  7.2 0.0 reduce-scatter.4.cloned.1.call-start
  7.2 3.0 %bitcast_convert_fusion = f32[1024,512]{1,0:T(8,128)} fusion(bf16[1,1024,512]{2,1,0:T(8,128)(2,1)} %param.11), kind=kLoop, calls=%fused_computation.23 | loop fusion | flops 524288 | bytes 3145728 | tf_op jit(solution)/shard_map/convert_element_type | solution.py:48
  10.3 1.4 copy.15
  11.7 1.2 copy.62
  12.9 0.1 broadcast_in_dim.33
  13.0 1.9 pad_maximum_fusion
  14.8 5.0 %all-to-all-start = ((bf16[8,128,1536]{2,1,0:T(8,128)(2,1)}), bf16[8,128,1536]{2,1,0:T(8,128)(2,1)S(1)}, u32[]{:S(2)}, u32[]{:S(2)}) async-start(bf16[8,128,1536]{2,1,0:T(8,128)(2,1)} %pad_maximum_fusion), calls=%async_computation | async-start | bytes 6291456 | tf_op jit(solution)/shard_map/all_to_all | solution.py:77
  19.9 0.0 reduce-scatter.6.cloned.1.call-start
  19.9 41.5 %reduce-scatter.4.cloned.1.call-done = f32[128,512]{1,0:T(8,128)} async-done(((f32[1024,512]{1,0:T(8,128)}), f32[128,512]{1,0:T(8,128)}) %reduce-scatter.4.cloned.1.call-update) | async-done | bytes 262160 | tf_op jit(solution)/shard_map/reduce_scatter | solution.py:50
  61.4 0.0 all-gather.5.cloned.1.call-start
  61.5 91.3 %reduce-scatter.6.cloned.1.call-done = f32[16,512]{1,0:T(8,128)} async-done(((f32[128,512]{1,0:T(8,128)}), f32[16,512]{1,0:T(8,128)}) %reduce-scatter.6.cloned.1.call-update) | async-done | bytes 32784 | tf_op jit(solution)/shard_map/reduce_scatter | solution.py:50
  152.8 1.4 fusion.31
  154.2 44.3 %all_gather.13 = bf16[128,512]{1,0:T(8,128)(2,1)} all-gather(bf16[16,512]{1,0:T(8,128)(2,1)S(1)} %get-tuple-element.5), channel_id=1, replica_groups=mesh['island0'=8,'island1'=4,'island2'=2,'fsdp'=8] {'island1','island2'}, dimensions={0}, use_global_device_ids=true | all-gather | bytes 147456 | tf_op jit(solution)/shard_map/all_gather | solution.py:56
  198.4 0.0 all-gather.5.cloned.1.call-update
  198.5 0.0 reduce-scatter.8.cloned.1.call-start
  198.5 2.1 multiply_reduce_fusion
  200.6 9.3 %all-gather.2 = f32[8,1,128]{2,1,0:T(1,128)S(1)} all-gather(f32[1,1,128]{2,1,0:T(1,128)S(1)} %rsqrt_bitcast_fusion), channel_id=2, replica_groups=mesh['island0'=8,'island1'=4,'island2'=2,'fsdp'=8] {'fsdp'}, dimensions={0}, use_global_device_ids=true | all-gather | bytes 4608 | tf_op jit(solution)/shard_map/all_gather | solution.py:83
  209.9 9.7 %all-gather.1 = s32[1,1024]{1,0:T(1,128)S(1)} all-gather(s32[1,128]{1,0:T(1,128)S(1)} %copy-done.11), channel_id=3, replica_groups=mesh['island0'=8,'island1'=4,'island2'=2,'fsdp'=8] {'fsdp'}, dimensions={1}, use_global_device_ids=true | all-gather | bytes 4608 | tf_op jit(solution)/shard_map/all_gather | solution.py:60
  219.6 0.1 select_reduce_fusion.1
  219.7 0.1 select_reduce_fusion
  219.8 0.3 slice.120
  220.1 1.3 copy-done.2
  221.4 1.9 fusion.2
  223.3 15.5 %all-gather.5.cloned.1.call-done = bf16[1024,512]{1,0:T(8,128)(2,1)} async-done(((bf16[128,512]{1,0:T(8,128)(2,1)}), bf16[1024,512]{1,0:T(8,128)(2,1)}) %all-gather.5.cloned.1.call-update) | async-done | bytes 1048592 | tf_op jit(solution)/shard_map/all_gather | solution.py:56
  238.8 4.4 %fusion.32 = f32[1024,512]{1,0:T(8,128)} fusion(bf16[1024,1024]{1,0:T(8,128)(2,1)} %fusion.2, bf16[1024,512]{1,0:T(8,128)(2,1)} %all-gather.5.cloned.1.call-done), kind=kOutput, calls=%fused_computation.74 | convolution fusion | flops 1073741824 | bytes 5242880 | tf_op jit(solution)/shard_map/dot_general | solution.py:98
  243.2 3.0 %broadcast_multiply_fusion = (f32[1024,64]{1,0:T(8,128)}, f32[1024,64]{1,0:T(8,128)S(1)}, f32[1024,64]{1,0:T(8,128)S(1)}) fusion(f32[64]{0:T(128)S(1)} %multiply_exponential_fusion, f32[1024]{0:T(1024)S(1)} %subtract_convert_fusion.2), kind=kLoop, calls=%fused_computation.34 | loop fusion | flops 131072 | bytes 790784 | tf_op jit(solution)/shard_map/mul | solution.py:35
  246.2 0.8 copy-done.4
  247.0 1.6 slice_convert_fusion
  248.6 2.0 reshape.137
  250.7 1.6 subtract_convert_fusion
  252.3 0.7 slice_maximum_fusion.3
  253.0 0.7 slice_maximum_fusion.7
  253.8 1.4 pad_maximum_fusion.2
  255.2 0.2 copy-done
  255.3 0.5 convolution_convert_fusion.6
  255.8 0.5 convolution_convert_fusion
  256.3 0.4 convolution_convert_fusion.1
  256.7 0.4 convolution_convert_fusion.2
  257.2 0.4 convolution_convert_fusion.3
  257.6 0.4 convolution_convert_fusion.5
  258.1 0.4 convolution_convert_fusion.4
  258.6 2.2 fusion.4
  260.7 1.9 fusion.3
  262.6 22.8 %reduce-scatter.8.cloned.1.call-done = f32[128,512]{1,0:T(8,128)} async-done(((f32[1024,512]{1,0:T(8,128)}), f32[128,512]{1,0:T(8,128)}) %reduce-scatter.8.cloned.1.call-update) | async-done | bytes 262160 | tf_op jit(solution)/shard_map/reduce_scatter | solution.py:99
  285.4 1.0 reshape.134
  286.5 0.3 subtract_convert_fusion.1
  286.7 0.2 pad_maximum_fusion.1
  286.9 0.7 convert_element_type.114
  (32 shorter events, 0.1 us)
Async XLA Ops:
  7.2 3.1 %copy-start.1 = (bf16[1,128,8192]{2,1,0:T(8,128)(2,1)S(1)}, bf16[1,128,8192]{2,1,0:T(8,128)(2,1)}, u32[]{:S(2)}) copy-start(bf16[1,128,8192]{2,1,0:T(8,128)(2,1)} %param.7) | copy-start | bytes 6291460
  7.2 54.2 %reduce-scatter.4.cloned.1.call-start = ((), (), s32[]{:S(2)}) async-start(), calls=%async_computation.4 | async-start | bytes 2359296 | tf_op jit(solution)/shard_map/reduce_scatter | solution.py:50
  11.7 1.2 copy-start.7
  14.8 137.9 %copy-start.8 = (f32[16,512]{1,0:T(8,128)S(1)}, f32[16,512]{1,0:T(8,128)}, u32[]{:S(2)}) copy-start(f32[16,512]{1,0:T(8,128)} %param.12) | copy-start | bytes 98308
  14.8 137.9 %copy-start.9 = (f32[16,512]{1,0:T(8,128)S(1)}, f32[16,512]{1,0:T(8,128)}, u32[]{:S(2)}) copy-start(f32[16,512]{1,0:T(8,128)} %param.13) | copy-start | bytes 98308
  14.8 183.7 %copy-start.10 = (bf16[1024]{0:T(1024)(128)(2,1)S(1)}, bf16[1024]{0:T(1024)(128)(2,1)}, u32[]{:S(2)}) copy-start(bf16[1024]{0:T(1024)(128)(2,1)} %param.8) | copy-start | bytes 6148
  14.8 205.0 %all-to-all-start = ((bf16[8,128,1536]{2,1,0:T(8,128)(2,1)}), bf16[8,128,1536]{2,1,0:T(8,128)(2,1)S(1)}, u32[]{:S(2)}, u32[]{:S(2)}) async-start(bf16[8,128,1536]{2,1,0:T(8,128)(2,1)} %pad_maximum_fusion), calls=%async_computation | async-start | bytes 6291456 | tf_op jit(solution)/shard_map/all_to_all | solution.py:77
  19.9 190.1 %copy-start.11 = (s32[1,128]{1,0:T(1,128)S(1)}, s32[1,128]{1,0:T(1,128)}, u32[]{:S(2)}) copy-start(s32[1,128]{1,0:T(1,128)} %param.9) | copy-start | bytes 1540
  19.9 132.9 %reduce-scatter.6.cloned.1.call-start = ((), (), s32[]{:S(2)}) async-start(), calls=%async_computation.5 | async-start | bytes 294912 | tf_op jit(solution)/shard_map/reduce_scatter | solution.py:50
  61.4 177.4 %all-gather.5.cloned.1.call-start = ((), (), s32[]{:S(2)}) async-start(), calls=%async_computation.6 | async-start | bytes 1179648 | tf_op jit(solution)/shard_map/all_gather | solution.py:56
  198.5 87.0 %reduce-scatter.8.cloned.1.call-start = ((), (), s32[]{:S(2)}) async-start(), calls=%async_computation.7 | async-start | bytes 2359296 | tf_op jit(solution)/shard_map/reduce_scatter | solution.py:99
  220.1 1.3 copy-start.2
  246.2 0.8 copy-start.4
  248.6 2.0 copy-start.5
  248.6 2.0 copy-start.6
  253.8 1.6 copy-start
  258.5 2.2 copy-start.3
  258.6 2.2 copy-start.12
Sparse Core Ops, SparseCore 0:
  10.8 50.5 reduce-scatter.3
  65.8 86.9 reduce-scatter.5
  198.6 40.1 all-gather.4
  243.3 42.0 reduce-scatter.7
where the time goes:
time: 295 us; the launch traced here: 294 us
  waiting for transfers between devices  171 us (58%)
  blocking collectives  63.2 us (21%)
  other arithmetic  20 us (7%)
  between operations  14 us (5%)
  matrix products  11.6 us (4%)
  local copies, waits for them, and re-layouts  9 us (3%)
  starting transfers between devices  5.17 us (2%)
    reduce_scatter x2, waiting for transfers between devices, body(): summed = lax.psum_scatter(summed, axes, scatter_dimension=0, tiled=True)  133 us
    all_gather x1, blocking collectives, body(): weight_shard = lax.all_gather(weight_shard, axes, axis=0, tiled=True)  44.3 us
    reduce_scatter x1, waiting for transfers between devices, body(): lax.psum_scatter(partial_keys, 'fsdp', scatter_dimension=0, tiled=True)  22.8 us
    all_gather x1, waiting for transfers between devices, body(): weight_shard = lax.all_gather(weight_shard, axes, axis=0, tiled=True)  15.5 us
    all_gather x1, blocking collectives, body(): all_docs = lax.all_gather(doc_ids[0], 'fsdp', axis=0, tiled=True)  9.69 us
    all_gather x1, blocking collectives, body(): all_scales = lax.all_gather(row_scale, 'fsdp', axis=0, tiled=True)  9.28 us
  transfers between devices with their start and end apart: 5, of which 4 were waited for; matrix products, arithmetic and copies ran while one was open for 10% of the time, Pallas kernels for 0%

commit v1 on v0

--- a/solution.py
+++ b/solution.py
@@ -14,6 +14,13 @@
 rope_base = 500000.0
 far_index = 1 << 30
 ISLAND_FACTORS = None
+
+
+def gather_over(shard, axis, dim):
+    peers = lax.axis_size(axis)
+    blocks = jnp.stack([shard for _ in range(peers)])
+    blocks = lax.all_to_all(blocks, axis, split_axis=0, concat_axis=0)
+    return jnp.concatenate(blocks, axis=dim)
 
 
 def angles_for(positions, head_width):
@@ -57,7 +64,7 @@
     tok_rows = hidden.shape[1]
     seq = tok_rows * fsdp_ways
     me = lax.axis_index("fsdp")
-    all_docs = lax.all_gather(doc_ids[0], "fsdp", axis=0, tiled=True)
+    all_docs = gather_over(doc_ids[0], "fsdp", 0)
     indices = jnp.arange(seq, dtype=jnp.int32)
     documents = jnp.arange(DOCS, dtype=jnp.int32)
     in_document = all_docs[:, None] == documents[None, :]

time: 295 us -> 297 us (level)
  blocking collectives: 63.2 us -> 53.7 us
  waiting for transfers between devices: 171 us -> 179 us
  starting transfers between devices: 5.17 us -> 9.35 us
    all_gather x1 -> x0, blocking collectives: 9.69 us -> none  [body(): all_docs = lax.all_gather(doc_ids[0], 'fsdp', axis=0, tiled=True)]
    all_gather x1, waiting for transfers between devices: 15.5 us -> 25 us  [body(): weight_shard = lax.all_gather(weight_shard, axes, axis=0, tiled=True)]
    all_to_all x0 -> x1, starting transfers between devices: none -> 4.88 us  [gather_over(): blocks = lax.all_to_all(blocks, axis, split_axis=0, concat_axis=0)]
    reduce_scatter x2, waiting for transfers between devices: 133 us -> 130 us  [body(): summed = lax.psum_scatter(summed, axes, scatter_dimension=0, tiled=True)]
  transfers between devices with their start and end apart: 5 -> 6, of which waited for: 4 -> 5; matrix products, arithmetic and copies ran while one was open for 10% -> 10% of each run, Pallas kernels for 0% -> 0%
where the time goes in v1:
time: 297 us
  waiting for transfers between devices  179 us (60%)
  blocking collectives  53.7 us (18%)
  other arithmetic  20 us (7%)
  between operations  14 us (5%)
  matrix products  11.6 us (4%)
  local copies, waits for them, and re-layouts  9.6 us (3%)
  starting transfers between devices  9.35 us (3%)
    reduce_scatter x2, waiting for transfers between devices, body(): summed = lax.psum_scatter(summed, axes, scatter_dimension=0, tiled=True)  130 us
    all_gather x1, blocking collectives, body(): weight_shard = lax.all_gather(weight_shard, axes, axis=0, tiled=True)  44.3 us
    all_gather x1, waiting for transfers between devices, body(): weight_shard = lax.all_gather(weight_shard, axes, axis=0, tiled=True)  25 us
    reduce_scatter x1, waiting for transfers between devices, body(): lax.psum_scatter(partial_keys, 'fsdp', scatter_dimension=0, tiled=True)  22.7 us
    all_gather x1, blocking collectives, body(): all_scales = lax.all_gather(row_scale, 'fsdp', axis=0, tiled=True)  9.44 us
  transfers between devices with their start and end apart: 6, of which 5 were waited for; matrix products, arithmetic and copies ran while one was open for 10% of the time, Pallas kernels for 0%

profile of v1, /device:TPU:6, one launch (start us, length us, event | category | flops | bytes accessed | tf_op | source)
XLA Modules:
  0.0 296.9 jit_solution(6862281156615100563)
XLA Ops:
  7.2 0.0 reduce-scatter.4.cloned.1.call-start
  7.2 3.0 %bitcast_convert_fusion = f32[1024,512]{1,0:T(8,128)} fusion(bf16[1,1024,512]{2,1,0:T(8,128)(2,1)} %param.11), kind=kLoop, calls=%fused_computation.23 | loop fusion | flops 524288 | bytes 3145728 | tf_op jit(solution)/shard_map/convert_element_type | solution.py:55
  10.3 0.6 stack.3
  10.9 4.9 %all-to-all-start.1 = ((s32[8,1,128]{2,1,0:T(1,128)}), s32[8,1,128]{2,1,0:T(1,128)S(1)}, u32[]{:S(2)}, u32[]{:S(2)}) async-start(s32[8,1,128]{2,1,0:T(1,128)} %stack.3), calls=%async_computation.4 | async-start | bytes 8192 | tf_op jit(solution)/shard_map/all_to_all | solution.py:22
  15.8 1.4 copy.15
  17.2 1.2 copy.62
  18.4 0.1 broadcast_in_dim.50
  18.5 1.9 pad_maximum_fusion
  20.3 0.9 all-to-all-done.1
  21.3 4.3 %all-to-all-start = ((bf16[8,128,1536]{2,1,0:T(8,128)(2,1)}), bf16[8,128,1536]{2,1,0:T(8,128)(2,1)S(1)}, u32[]{:S(2)}, u32[]{:S(2)}) async-start(bf16[8,128,1536]{2,1,0:T(8,128)(2,1)} %pad_maximum_fusion), calls=%async_computation | async-start | bytes 6291456 | tf_op jit(solution)/shard_map/all_to_all | solution.py:84
  25.6 35.8 %reduce-scatter.4.cloned.1.call-done = f32[128,512]{1,0:T(8,128)} async-done(((f32[1024,512]{1,0:T(8,128)}), f32[128,512]{1,0:T(8,128)}) %reduce-scatter.4.cloned.1.call-update) | async-done | bytes 262160 | tf_op jit(solution)/shard_map/reduce_scatter | solution.py:57
  61.4 0.0 all-gather.4.cloned.1.call-start
  61.5 94.0 %reduce-scatter.6.cloned.1.call-done = f32[16,512]{1,0:T(8,128)} async-done(((f32[128,512]{1,0:T(8,128)}), f32[16,512]{1,0:T(8,128)}) %reduce-scatter.6.cloned.1.call-update) | async-done | bytes 32784 | tf_op jit(solution)/shard_map/reduce_scatter | solution.py:57
  155.5 1.4 fusion.31
  156.9 44.3 %all_gather.10 = bf16[128,512]{1,0:T(8,128)(2,1)} all-gather(bf16[16,512]{1,0:T(8,128)(2,1)S(1)} %get-tuple-element.5), channel_id=1, replica_groups=mesh['island0'=8,'island1'=4,'island2'=2,'fsdp'=8] {'island1','island2'}, dimensions={0}, use_global_device_ids=true | all-gather | bytes 147456 | tf_op jit(solution)/shard_map/all_gather | solution.py:63
  201.2 0.0 reduce-scatter.8.cloned.1.call-start
  201.3 2.1 multiply_reduce_fusion
  203.4 9.4 %all-gather.1 = f32[8,1,128]{2,1,0:T(1,128)S(1)} all-gather(f32[1,1,128]{2,1,0:T(1,128)S(1)} %rsqrt_bitcast_fusion), channel_id=2, replica_groups=mesh['island0'=8,'island1'=4,'island2'=2,'fsdp'=8] {'fsdp'}, dimensions={0}, use_global_device_ids=true | all-gather | bytes 4608 | tf_op jit(solution)/shard_map/all_gather | solution.py:90
  212.8 0.1 select_reduce_fusion.1
  212.9 0.1 select_reduce_fusion
  213.0 0.3 slice.120
  213.3 1.3 copy-done.2
  214.6 1.9 fusion.2
  216.5 25.0 %all-gather.4.cloned.1.call-done = bf16[1024,512]{1,0:T(8,128)(2,1)} async-done(((bf16[128,512]{1,0:T(8,128)(2,1)}), bf16[1024,512]{1,0:T(8,128)(2,1)}) %all-gather.4.cloned.1.call-update) | async-done | bytes 1048592 | tf_op jit(solution)/shard_map/all_gather | solution.py:63
  241.6 4.4 %fusion.32 = f32[1024,512]{1,0:T(8,128)} fusion(bf16[1024,1024]{1,0:T(8,128)(2,1)} %fusion.2, bf16[1024,512]{1,0:T(8,128)(2,1)} %all-gather.4.cloned.1.call-done), kind=kOutput, calls=%fused_computation.74 | convolution fusion | flops 1073741824 | bytes 5242880 | tf_op jit(solution)/shard_map/dot_general | solution.py:105
  246.0 3.0 %broadcast_multiply_fusion = (f32[1024,64]{1,0:T(8,128)}, f32[1024,64]{1,0:T(8,128)S(1)}, f32[1024,64]{1,0:T(8,128)S(1)}) fusion(f32[64]{0:T(128)S(1)} %multiply_exponential_fusion, f32[1024]{0:T(1024)S(1)} %subtract_convert_fusion.2), kind=kLoop, calls=%fused_computation.34 | loop fusion | flops 131072 | bytes 790784 | tf_op jit(solution)/shard_map/mul | solution.py:42
  249.0 0.8 copy-done.4
  249.8 1.6 slice_convert_fusion
  251.4 2.0 reshape.145
  253.5 1.6 subtract_convert_fusion
  255.1 0.7 slice_maximum_fusion.3
  255.8 0.7 slice_maximum_fusion.7
  256.5 1.4 pad_maximum_fusion.2
  258.0 0.2 copy-done
  258.1 0.5 convolution_convert_fusion.6
  258.6 0.5 convolution_convert_fusion
  259.0 0.5 convolution_convert_fusion.1
  259.5 0.5 convolution_convert_fusion.2
  260.0 0.4 convolution_convert_fusion.3
  260.4 0.4 convolution_convert_fusion.5
  260.9 0.4 convolution_convert_fusion.4
  261.3 2.2 fusion.4
  263.5 1.9 fusion.3
  265.4 22.7 %reduce-scatter.8.cloned.1.call-done = f32[128,512]{1,0:T(8,128)} async-done(((f32[1024,512]{1,0:T(8,128)}), f32[128,512]{1,0:T(8,128)}) %reduce-scatter.8.cloned.1.call-update) | async-done | bytes 262160 | tf_op jit(solution)/shard_map/reduce_scatter | solution.py:106
  288.2 1.0 reshape.142
  289.2 0.3 subtract_convert_fusion.1
  289.5 0.2 pad_maximum_fusion.1
  289.7 0.7 convert_element_type.114
  (34 shorter events, 0.2 us)
Async XLA Ops:
  7.2 3.1 %copy-start.11 = (s32[1,128]{1,0:T(1,128)S(1)}, s32[1,128]{1,0:T(1,128)}, u32[]{:S(2)}) copy-start(s32[1,128]{1,0:T(1,128)} %param.9) | copy-start | bytes 1540
  7.2 8.6 %copy-start.1 = (bf16[1,128,8192]{2,1,0:T(8,128)(2,1)S(1)}, bf16[1,128,8192]{2,1,0:T(8,128)(2,1)}, u32[]{:S(2)}) copy-start(bf16[1,128,8192]{2,1,0:T(8,128)(2,1)} %param.7) | copy-start | bytes 6291460
  7.2 54.2 %reduce-scatter.4.cloned.1.call-start = ((), (), s32[]{:S(2)}) async-start(), calls=%async_computation.5 | async-start | bytes 2359296 | tf_op jit(solution)/shard_map/reduce_scatter | solution.py:57
  10.9 10.4 %all-to-all-start.1 = ((s32[8,1,128]{2,1,0:T(1,128)}), s32[8,1,128]{2,1,0:T(1,128)S(1)}, u32[]{:S(2)}, u32[]{:S(2)}) async-start(s32[8,1,128]{2,1,0:T(1,128)} %stack.3), calls=%async_computation.4 | async-start | bytes 8192 | tf_op jit(solution)/shard_map/all_to_all | solution.py:22
  17.2 1.2 copy-start.7
  20.3 135.2 %copy-start.8 = (f32[16,512]{1,0:T(8,128)S(1)}, f32[16,512]{1,0:T(8,128)}, u32[]{:S(2)}) copy-start(f32[16,512]{1,0:T(8,128)} %param.12) | copy-start | bytes 98308
  20.3 135.2 %copy-start.9 = (f32[16,512]{1,0:T(8,128)S(1)}, f32[16,512]{1,0:T(8,128)}, u32[]{:S(2)}) copy-start(f32[16,512]{1,0:T(8,128)} %param.13) | copy-start | bytes 98308
  20.3 180.9 %copy-start.10 = (bf16[1024]{0:T(1024)(128)(2,1)S(1)}, bf16[1024]{0:T(1024)(128)(2,1)}, u32[]{:S(2)}) copy-start(bf16[1024]{0:T(1024)(128)(2,1)} %param.8) | copy-start | bytes 6148
  21.3 191.8 %all-to-all-start = ((bf16[8,128,1536]{2,1,0:T(8,128)(2,1)}), bf16[8,128,1536]{2,1,0:T(8,128)(2,1)S(1)}, u32[]{:S(2)}, u32[]{:S(2)}) async-start(bf16[8,128,1536]{2,1,0:T(8,128)(2,1)} %pad_maximum_fusion), calls=%async_computation | async-start | bytes 6291456 | tf_op jit(solution)/shard_map/all_to_all | solution.py:84
  25.6 129.9 %reduce-scatter.6.cloned.1.call-start = ((), (), s32[]{:S(2)}) async-start(), calls=%async_computation.6 | async-start | bytes 294912 | tf_op jit(solution)/shard_map/reduce_scatter | solution.py:57
  61.4 180.1 %all-gather.4.cloned.1.call-start = ((), (), s32[]{:S(2)}) async-start(), calls=%async_computation.7 | async-start | bytes 1179648 | tf_op jit(solution)/shard_map/all_gather | solution.py:63
  201.2 87.0 %reduce-scatter.8.cloned.1.call-start = ((), (), s32[]{:S(2)}) async-start(), calls=%async_computation.8 | async-start | bytes 2359296 | tf_op jit(solution)/shard_map/reduce_scatter | solution.py:106
  213.3 1.3 copy-start.2
  249.0 0.8 copy-start.4
  251.4 2.0 copy-start.5
  251.4 2.0 copy-start.6
  256.5 1.6 copy-start
  261.3 2.2 copy-start.3
  261.3 2.2 copy-start.12
Sparse Core Ops, SparseCore 0:
  10.8 50.5 reduce-scatter.3
  65.8 89.6 reduce-scatter.5
  201.3 40.2 all-gather.3
  246.1 41.9 reduce-scatter.7
